TPU v7x, 512 devices: a whole 4x8x8 slice. The times are simulated.
512 devices in a mesh: rows: 32 (over y, x), vocab: 16 (over z, core).
Axes of the slice: x: 4, y: 8, z: 8, core: 2. Of those that a mesh axis runs over, the one named last changes fastest.
Arguments:
- hidden: bfloat16 [12288, 8192], P('rows', 'vocab'), may hold values from -128 to 128
- head: bfloat16 [8192, 8192], P('rows', 'vocab'), may hold values from -4 to 4
- targets: int32 [12288], P('rows'), may hold values from 0 to 128255
- live: int32 [12288], P('rows'), may hold values from 0 to 1, as said below
- prior_lse: float32 [12288], P('rows'), may hold values from 10 to 18
- prior_mean: float32 [12288], P('rows'), may hold values from 2 to 8
- prior_target: float32 [12288], P('rows'), may hold values from -12 to 12
- seq_lengths: int32 [32], replicated, may hold values from 1 to 768, 12288 in all
Outputs:
- logprob: float32 [12288], P(('rows', 'vocab'))
- entropy: float32 [12288], P(('rows', 'vocab'))
- seq_score: float32 [32], replicated
Inputs may be any that keep to these rules, and one draw needn't show every extreme that they name: Within the 384 rows of each index of rows, the live rows come first; every such index has at least 48 live rows and some index has all 384.
All inputs are finite; a program needn't handle non-finite values.
Results may differ from a plain program's by a relative error of at most 0.0003.
Values may be sent and summed in bfloat16 or wider, within the bound.
No kernel may reach another device: no remote copies, remote signals or barrier semaphores. Data moves between devices by JAX's collectives and lax.ppermute only.
A program may use at most 64 MiB of HBM per device.

v0:
```python
import jax
import jax.numpy as jnp
from jax import lax
from jax.sharding import PartitionSpec as P

VOCAB = 128256
SEQS = 32
GSIZE = 8


def finish_rows(block_peak, block_mass, block_moment, block_target, live, prior_lse, prior_mean):
    highest = jnp.maximum(block_peak, prior_lse)
    earlier = jnp.exp(prior_lse - highest)
    scaled = jnp.exp(block_peak - highest)
    total_mass = earlier + block_mass * scaled
    norm_log = highest + jnp.log(total_mass)
    average = (earlier * prior_mean + scaled * block_moment) / total_mass
    keeping = live.astype(jnp.float32)
    return (keeping * (block_target - norm_log), keeping * (norm_log - average))


def local(hidden, head, targets, live, prior_lse, prior_mean, prior_target, seq_lengths):
    rows_here = hidden.shape[0]
    cols_here = head.shape[1]
    spread = lax.axis_size("vocab")
    which = lax.axis_index("vocab")
    block_first = VOCAB - cols_here * spread
    first_col = block_first + which * cols_here
    gathered = lax.all_gather(hidden, "vocab", axis=1, tiled=True)
    logits = jnp.dot(
        gathered,
        lax.all_gather(head, "rows", axis=0, tiled=True),
        preferred_element_type=jnp.float32,
    )
    row_peak = jnp.max(logits, axis=1)
    weights = jnp.exp(logits - row_peak[:, None])
    row_mass = jnp.sum(weights, axis=1)
    moment = jnp.sum(weights * logits, axis=1)
    column = targets - first_col
    columns = lax.broadcasted_iota(jnp.int32, logits.shape, 1)
    picked = jnp.sum(jnp.where(columns == column[:, None], logits, jnp.zeros_like(logits)), axis=1)
    share = rows_here // spread
    begin = which * share

    def own_rows(values):
        return lax.dynamic_slice_in_dim(values, begin, share, 0)

    highest = lax.pmax(row_peak, "vocab")
    factor = jnp.exp(row_peak - highest)
    mass_all, moment_all, picked_all = lax.psum(
        (row_mass * factor, moment * factor, picked), "vocab"
    )
    peak_share = own_rows(highest)
    mass_share = own_rows(mass_all)
    moment_share = own_rows(moment_all)
    picked_share = own_rows(picked_all)
    target_share = own_rows(targets)
    block_target = jnp.where(target_share >= block_first, picked_share, own_rows(prior_target))
    logprob, entropy = finish_rows(
        peak_share,
        mass_share,
        moment_share,
        block_target,
        own_rows(live),
        own_rows(prior_lse),
        own_rows(prior_mean),
    )
    global_rows = lax.axis_index("rows") * rows_here + begin + jnp.arange(share, dtype=jnp.int32)
    endings = jnp.cumsum(seq_lengths)
    member = jnp.sum((global_rows[:, None] >= endings[None, :]).astype(jnp.int32), axis=1)
    onehot = (member[:, None] == jnp.arange(SEQS, dtype=jnp.int32)[None, :]).astype(jnp.float32)
    partial_sums = jnp.sum(onehot * logprob[:, None], axis=0)
    sums = lax.psum(partial_sums, ("rows", "vocab"))
    seq_mean = sums / seq_lengths.astype(jnp.float32)
    grouped = seq_mean.reshape(SEQS // GSIZE, GSIZE)
    seq_score = (grouped - jnp.mean(grouped, axis=1, keepdims=True)).reshape(SEQS)
    return (logprob, entropy, seq_score)


def solution(mesh):
    return jax.shard_map(
        local,
        mesh=mesh,
        in_specs=(
            P("rows", "vocab"),
            P("rows", "vocab"),
            P("rows"),
            P("rows"),
            P("rows"),
            P("rows"),
            P("rows"),
            P(),
        ),
        out_specs=(P(("rows", "vocab")), P(("rows", "vocab")), P()),
        check_vma=False,
    )
```

profile of v0, /device:TPU:1, one launch (start us, length us, event | category | flops | bytes accessed | tf_op | source)
XLA Modules:
  0.0 332.5 jit_solution(5648980550424565232)
XLA Ops:
  7.2 0.0 all-gather.3.cloned.1.call-start
  7.2 0.7 all-gather.3.cloned.1.call-update
  7.9 0.0 all-gather.5.cloned.1.call-start
  7.9 0.7 all-gather.5.cloned.1.call-update
  8.7 0.7 copy.13
  9.4 0.1 reduce-window.8
  9.4 0.1 reduce
  9.6 0.2 convert_reduce_fusion
  9.8 0.7 broadcast_subtract_fusion
  10.4 0.0 copy-start
  10.4 55.1 %all-gather.3.cloned.1.call-done = bf16[384,8192]{1,0:T(8,128)(2,1)} async-done(((bf16[384,512]{1,0:T(8,128)(2,1)}), bf16[384,8192]{1,0:T(8,128)(2,1)}) %all-gather.3.cloned.1.call-update) | async-done | bytes 6291472 | tf_op jit(solution)/shard_map/all_gather | solution.py:29
  65.6 103.9 %all-gather.5.cloned.1.call-done = bf16[8192,512]{1,0:T(8,128)(2,1)} async-done(((bf16[256,512]{1,0:T(8,128)(2,1)}), bf16[8192,512]{1,0:T(8,128)(2,1)}) %all-gather.5.cloned.1.call-update) | async-done | bytes 8388624 | tf_op jit(solution)/shard_map/all_gather | solution.py:32
  169.4 8.0 %fusion.5 = (f32[384]{0:T(512)S(1)}, f32[384,512]{1,0:T(8,128)S(1)}) fusion(bf16[384,8192]{1,0:T(8,128)(2,1)} %all-gather.3.cloned.1.call-done, bf16[8192,512]{1,0:T(8,128)(2,1)} %all-gather.5.cloned.1.call-done), kind=kOutput, calls=%fused_computation.24 | convolution fusion | flops 3221421568 | bytes 15468032 | tf_op jit(solution)/shard_map/dot_general | solution.py:30
  177.4 25.1 %pmax.7 = f32[384]{0:T(512)S(1)} all-reduce(f32[384]{0:T(512)S(1)} %get-tuple-element.13), channel_id=1, replica_groups=mesh['rows'=32,'vocab'=16] {'vocab'}, use_global_device_ids=true, to_apply=%region_3.4 | all-reduce | flops 384 | bytes 3072 | tf_op jit(solution)/shard_map/pmax | solution.py:48
  202.5 0.5 multiply_reduce_fusion
  203.0 25.8 %all-reduce = (f32[384]{0:T(512)S(1)}, f32[384]{0:T(512)S(1)}, f32[384]{0:T(512)S(1)}) all-reduce(f32[384]{0:T(512)S(1)} %get-tuple-element.5, f32[384]{0:T(512)S(1)} %get-tuple-element.12, f32[384]{0:T(512)S(1)} %get-tuple-element.11), channel_id=1, replica_groups=mesh['rows'=32,'vocab'=16] {'vocab'}, use_global_device_ids=true, to_apply=%region_1.0 | all-reduce | flops 1152 | bytes 9216 | tf_op jit(solution)/shard_map/psum | solution.py:50
  228.9 1.4 subtract_multiply_fusion
  230.2 0.0 copy-start.1
  230.2 0.1 select_reduce_fusion.1
  230.3 94.4 %psum.31 = f32[32]{0:T(128)S(1)} all-reduce(f32[32]{0:T(128)S(1)} %select_reduce_fusion.1), channel_id=1, replica_groups=mesh['rows'=32,'vocab'=16] {'rows','vocab'}, use_global_device_ids=true, to_apply=%region_11.12 | all-reduce | flops 32 | bytes 256 | tf_op jit(solution)/shard_map/psum | solution.py:73
  324.7 0.0 copy-done
  324.7 0.1 reshape.49
  324.8 0.1 reduce_sum.59
  325.0 0.1 sub.49
  325.0 0.1 sub.50
  325.1 0.5 sub.51
  325.6 0.0 copy-done.1
  (4 shorter events, 0.0 us)
Async XLA Ops:
  7.2 58.4 %all-gather.3.cloned.1.call-start = ((), (), s32[]{:S(2)}) async-start(), calls=%async_computation | async-start | bytes 6684672 | tf_op jit(solution)/shard_map/all_gather | solution.py:29
  7.9 161.5 %all-gather.5.cloned.1.call-start = ((), (), s32[]{:S(2)}) async-start(), calls=%async_computation.1 | async-start | bytes 8650752 | tf_op jit(solution)/shard_map/all_gather | solution.py:32
  10.4 314.3 %copy-start = (s32[32]{0:T(128)S(1)}, s32[32]{0:T(128)}, u32[]{:S(2)}) copy-start(s32[32]{0:T(128)} %param.15) | copy-start | bytes 388
  230.2 95.4 %copy-start.1 = (f32[24]{0:T(128)}, f32[24]{0:T(128)S(1)}, u32[]{:S(2)}) copy-start(f32[24]{0:T(128)S(1)} %get-tuple-element.10) | copy-start | bytes 292
Sparse Core Ops, SparseCore 0:
  10.1 55.3 all-gather.2
  68.7 100.6 all-gather.4
where the time goes:
time: 333 us; the launch traced here: 332 us
  waiting for transfers between devices  160 us (48%)
  blocking collectives  145 us (44%)
  between operations  14.1 us (4%)
  matrix products  8 us (2%)
  other arithmetic  3.64 us (1%)
    all_gather x1, waiting for transfers between devices, local(): lax.all_gather(head, 'rows', axis=0, tiled=True)  104 us
    psum x1, blocking collectives, local(): sums = lax.psum(partial_sums, ('rows', 'vocab'))  94.4 us
    all_gather x1, waiting for transfers between devices, local(): gathered = lax.all_gather(hidden, 'vocab', axis=1, tiled=True)  55.1 us
    psum x1, blocking collectives, local(): lax.psum((row_mass * factor, moment * factor, picked), 'vocab')  25.8 us
    pmax x1, blocking collectives, local(): highest = lax.pmax(row_peak, 'vocab')  25.1 us
    dot_general x1, matrix products, local(): jnp.dot(gathered, lax.all_gather(head, 'rows', axis=0, tiled=True), prefe...  8 us
  transfers between devices with their start and end apart: 2, of which 2 were waited for; matrix products, arithmetic and copies ran while one was open for 1% of the time, Pallas kernels for 0%

commit v1 on v0

--- a/solution.py
+++ b/solution.py
@@ -70,7 +70,7 @@
     member = jnp.sum((global_rows[:, None] >= endings[None, :]).astype(jnp.int32), axis=1)
     onehot = (member[:, None] == jnp.arange(SEQS, dtype=jnp.int32)[None, :]).astype(jnp.float32)
     partial_sums = jnp.sum(onehot * logprob[:, None], axis=0)
-    sums = lax.psum(partial_sums, ("rows", "vocab"))
+    sums = jnp.sum(lax.all_gather(partial_sums, ("rows", "vocab")), axis=0)
     seq_mean = sums / seq_lengths.astype(jnp.float32)
     grouped = seq_mean.reshape(SEQS // GSIZE, GSIZE)
     seq_score = (grouped - jnp.mean(grouped, axis=1, keepdims=True)).reshape(SEQS)

time: 333 us -> 494 us (1.48)
  waiting for transfers between devices: 160 us -> 415 us
  blocking collectives: 145 us -> 50.9 us
    unnamed x2 -> x4, waiting for transfers between devices: 1.38 us -> 256 us
    psum x1 -> x0, blocking collectives: 94.4 us -> none  [local(): sums = lax.psum(partial_sums, ('rows', 'vocab'))]
  transfers between devices with their start and end apart: 2 -> 3, of which waited for: 2 -> 3; matrix products, arithmetic and copies ran while one was open for 1% -> 0% of each run, Pallas kernels for 0% -> 0%
where the time goes in v1:
time: 494 us
  waiting for transfers between devices  415 us (84%)
  blocking collectives  50.9 us (10%)
  between operations  13.8 us (3%)
  matrix products  8 us (2%)
    unnamed x4, waiting for transfers between devices  256 us
    all_gather x1, waiting for transfers between devices, local(): lax.all_gather(head, 'rows', axis=0, tiled=True)  104 us
    all_gather x1, waiting for transfers between devices, local(): gathered = lax.all_gather(hidden, 'vocab', axis=1, tiled=True)  55 us
    psum x1, blocking collectives, local(): lax.psum((row_mass * factor, moment * factor, picked), 'vocab')  25.8 us
    pmax x1, blocking collectives, local(): highest = lax.pmax(row_peak, 'vocab')  25.1 us
  transfers between devices with their start and end apart: 3, of which 3 were waited for; matrix products, arithmetic and copies ran while one was open for 0% of the time, Pallas kernels for 0%

profile of v1, /device:TPU:1, one launch (start us, length us, event | category | flops | bytes accessed | tf_op | source)
XLA Modules:
  0.0 494.0 jit_solution(16859396387170751881)
XLA Ops:
  7.2 0.0 all-gather.4.cloned.1.call-start
  7.2 0.7 all-gather.4.cloned.1.call-update
  7.9 0.0 all-gather.6.cloned.1.call-start
  7.9 0.7 all-gather.6.cloned.1.call-update
  8.6 0.0 all-reduce.4.cloned.1.call-start
  8.7 0.7 copy.13
  9.4 0.1 reduce-window.8
  9.5 0.1 reduce
  9.6 0.2 convert_reduce_fusion
  9.8 0.7 broadcast_subtract_fusion
  10.5 0.0 copy-start.1
  10.5 55.0 %all-gather.4.cloned.1.call-done = bf16[384,8192]{1,0:T(8,128)(2,1)} async-done(((bf16[384,512]{1,0:T(8,128)(2,1)}), bf16[384,8192]{1,0:T(8,128)(2,1)}) %all-gather.4.cloned.1.call-update) | async-done | bytes 6291472 | tf_op jit(solution)/shard_map/all_gather | solution.py:29
  65.6 103.9 %all-gather.6.cloned.1.call-done = bf16[8192,512]{1,0:T(8,128)(2,1)} async-done(((bf16[256,512]{1,0:T(8,128)(2,1)}), bf16[8192,512]{1,0:T(8,128)(2,1)}) %all-gather.6.cloned.1.call-update) | async-done | bytes 8388624 | tf_op jit(solution)/shard_map/all_gather | solution.py:32
  169.4 8.0 %fusion.5 = (f32[384]{0:T(512)S(1)}, f32[384,512]{1,0:T(8,128)S(1)}) fusion(bf16[384,8192]{1,0:T(8,128)(2,1)} %all-gather.4.cloned.1.call-done, bf16[8192,512]{1,0:T(8,128)(2,1)} %all-gather.6.cloned.1.call-done), kind=kOutput, calls=%fused_computation.24 | convolution fusion | flops 3221421568 | bytes 15468032 | tf_op jit(solution)/shard_map/dot_general | solution.py:30
  177.4 25.1 %pmax.7 = f32[384]{0:T(512)S(1)} all-reduce(f32[384]{0:T(512)S(1)} %get-tuple-element.13), channel_id=1, replica_groups=mesh['rows'=32,'vocab'=16] {'vocab'}, use_global_device_ids=true, to_apply=%region_3.4 | all-reduce | flops 384 | bytes 3072 | tf_op jit(solution)/shard_map/pmax | solution.py:48
  202.5 0.5 multiply_reduce_fusion
  203.0 25.8 %all-reduce.1 = (f32[384]{0:T(512)S(1)}, f32[384]{0:T(512)S(1)}, f32[384]{0:T(512)S(1)}) all-reduce(f32[384]{0:T(512)S(1)} %get-tuple-element.5, f32[384]{0:T(512)S(1)} %get-tuple-element.12, f32[384]{0:T(512)S(1)} %get-tuple-element.11), channel_id=1, replica_groups=mesh['rows'=32,'vocab'=16] {'vocab'}, use_global_device_ids=true, to_apply=%region_1.0 | all-reduce | flops 1152 | bytes 9216 | tf_op jit(solution)/shard_map/psum | solution.py:50
  228.9 1.4 subtract_multiply_fusion
  230.2 0.1 select_reduce_fusion.1
  230.3 0.3 dynamic-update-slice
  230.6 0.6 copy-done
  231.2 0.0 all-reduce.4.cloned.1.call-update
  231.3 254.3 %all-reduce.4.cloned.1.call-done = f32[16384]{0:T(1024)} async-done(((f32[16384]{0:T(1024)}), f32[16384]{0:T(1024)}) %all-reduce.4.cloned.1.call-update) | async-done | bytes 65552
  485.5 0.9 reshape.50
  486.5 0.1 reduce_sum.68
  486.6 0.0 copy-done.1
  486.6 0.1 reshape.49
  486.7 0.1 reduce_sum.69
  486.8 0.1 sub.49
  486.9 0.1 sub.50
  487.0 0.5 sub.51
  487.5 0.0 copy-done.2
  (7 shorter events, 0.0 us)
Async XLA Ops:
  7.2 58.4 %all-gather.4.cloned.1.call-start = ((), (), s32[]{:S(2)}) async-start(), calls=%async_computation | async-start | bytes 6684672 | tf_op jit(solution)/shard_map/all_gather | solution.py:29
  7.9 161.5 %all-gather.6.cloned.1.call-start = ((), (), s32[]{:S(2)}) async-start(), calls=%async_computation.1 | async-start | bytes 8650752 | tf_op jit(solution)/shard_map/all_gather | solution.py:32
  8.6 476.9 %all-reduce.4.cloned.1.call-start = ((), (), s32[]{:S(2)}) async-start(), calls=%async_computation.2 | async-start | bytes 131072
  10.5 476.1 %copy-start.1 = (s32[32]{0:T(128)S(1)}, s32[32]{0:T(128)}, u32[]{:S(2)}) copy-start(s32[32]{0:T(128)} %param.15) | copy-start | bytes 388
  230.2 257.2 %copy-start.2 = (f32[24]{0:T(128)}, f32[24]{0:T(128)S(1)}, u32[]{:S(2)}) copy-start(f32[24]{0:T(128)S(1)} %get-tuple-element.10) | copy-start | bytes 292
  230.6 0.6 copy-start
Sparse Core Ops, SparseCore 0:
  10.1 55.3 all-gather.3
  68.7 100.6 all-gather.5
  231.4 254.1 all-reduce.3
